TPU v7x, 32 devices: a whole 2x2x4 slice. The times are simulated.
32 devices in a mesh: rep: 2 (over x), tm: 8 (over z, y), mp: 2 (over core).
Axes of the slice: x: 2, y: 2, z: 4, core: 2. Of those that a mesh axis runs over, the one named last changes fastest.
Arguments:
- inputs: bfloat16 [8, 1024, 1024], P('rep', 'tm'), parts along dimension 0, may hold values from -6 to 6
- resets: int32 [8, 1024], P('rep', 'tm'), parts along dimension 0, may hold values 0 or 1
- actions: int32 [8, 8, 128, 4], P('rep', None, 'tm'), parts along dimension 0, may hold values from 0 to 17
- in_proj: bfloat16 [1024, 1024], P(None, 'mp'), may hold values from -0.1875 to 0.1875
- decay_rates: float32 [1024], replicated, may hold values from 0.00024414062 to 0.03
- readout_w: bfloat16 [1024, 1024], P('mp'), may hold values from -0.1875 to 0.1875
- norm_gain: float32 [1024], replicated, may hold values from 0.1 to 1.9
- w_hidden: bfloat16 [1024, 1024], P(None, 'mp'), may hold values from -0.1875 to 0.1875
- action_embed: bfloat16 [18, 1024], P(None, 'mp'), may hold values from -6 to 6
- w_out: bfloat16 [1024, 1024], P('mp'), may hold values from -0.1875 to 0.1875
Outputs:
- predicted: bfloat16 [8, 8, 128, 4, 1024], P('rep', None, 'tm', None, 'mp'), parts along dimension 0
There are 2 independent parts, one for each index of `rep`. A program takes and returns all parts, laid end to end along the dimension named above; an argument that names none is the same for every part. Nothing has to cross between parts.
All inputs are finite; a program needn't handle non-finite values. No bound on the sum of `resets` on one device may be relied on, other than what follows from the above.
Results may differ from a plain program's by a relative error of at most 0.015.
Values may be sent and summed in bfloat16 or wider, within the bound.
No kernel may reach another device: no remote copies, remote signals or barrier semaphores. Data moves between devices by JAX's collectives and lax.ppermute only.
A program may use at most 64 MiB of HBM per device.

v0:
```python
import jax
import jax.numpy as jnp
from jax import lax
from jax.experimental import pallas as pl
from jax.experimental.pallas import tpu as pltpu
from jax.sharding import PartitionSpec as P


def _scan_kernel(x_ref, g_ref, o_ref):
    nb, steps, width = x_ref.shape

    def body(t, states):
        row = pl.ds(t, 1)
        new = []
        for b in range(nb):
            h = g_ref[b, row, :] * states[b] + x_ref[b, row, :]
            o_ref[b, row, :] = h
            new.append(h)
        return tuple(new)

    start = tuple(jnp.zeros((1, width), jnp.float32) for _ in range(nb))
    lax.fori_loop(0, steps, body, start, unroll=8)


def local_scan(driven, gates):
    size = driven.size
    return pl.pallas_call(
        _scan_kernel,
        out_shape=jax.ShapeDtypeStruct(driven.shape, jnp.float32),
        in_specs=[pl.BlockSpec(memory_space=pltpu.VMEM)] * 2,
        out_specs=pl.BlockSpec(memory_space=pltpu.VMEM),
        cost_estimate=pl.CostEstimate(flops=2 * size, bytes_accessed=12 * size, transcendentals=0),
    )(driven, gates)


def _scan_send_kernel(keep_ref, dec_ref, x_ref, send_ref, ends_ref, buf):
    nb, steps, width = x_ref.shape
    ntm, rows_sent, _ = send_ref.shape
    sub = rows_sent // nb
    dec = dec_ref[...]

    def body(t, states):
        row = pl.ds(t, 1)
        new = []
        for b in range(nb):
            h = (keep_ref[b, t] * dec) * states[b] + x_ref[b, row, :]
            buf[b, row, :] = h
            new.append(h)
        return tuple(new)

    start = tuple(jnp.zeros((1, width), jnp.float32) for _ in range(nb))
    final = lax.fori_loop(0, steps, body, start, unroll=8)
    for b in range(nb):
        ends_ref[pl.ds(b, 1), :] = final[b]
        for j in range(ntm):
            send_ref[j, pl.ds(b * sub, sub), pl.ds(0, width)] = buf[b, pl.ds(j * sub, sub), :].astype(
                jnp.bfloat16
            )


def scan_send(keep, decays, driven, ntm, spare):
    nb, steps, width = driven.shape
    sub = steps // ntm
    size = driven.size
    vmem = pl.BlockSpec(memory_space=pltpu.VMEM)
    return pl.pallas_call(
        _scan_send_kernel,
        out_shape=(
            jax.ShapeDtypeStruct((ntm, nb * sub, width + spare), jnp.bfloat16),
            jax.ShapeDtypeStruct((nb, width), jnp.float32),
        ),
        in_specs=[pl.BlockSpec(memory_space=pltpu.SMEM), vmem, vmem],
        out_specs=(vmem, vmem),
        scratch_shapes=[pltpu.VMEM((nb, steps, width), jnp.float32)],
        cost_estimate=pl.CostEstimate(flops=3 * size, bytes_accessed=6 * size, transcendentals=0),
    )(keep, decays.reshape(1, width), driven)


def gather_blocks(value, axis, mine, count):
    if count & (count - 1):
        return lax.all_gather(value, axis)
    held = value[None]
    shift = 1
    while shift < count:
        pairs = [(i, (i + shift) % count) for i in range(count)]
        held = jnp.concatenate([held, lax.ppermute(held, axis, pairs)], axis=0)
        shift *= 2
    order = (mine - jnp.arange(count, dtype=jnp.int32)) % count
    return jnp.take(held, order, axis=0)


def per_device(
    inputs,
    resets,
    actions,
    in_proj,
    decay_rates,
    readout_w,
    norm_gain,
    w_hidden,
    action_embed,
    w_out,
):
    m = lax.axis_index("mp")
    d = lax.axis_index("tm")
    ntm = lax.axis_size("tm")
    swap = [(0, 1), (1, 0)]

    def partner(x):
        return lax.ppermute(x, "mp", swap)

    half = in_proj.shape[1]
    ip_o = partner(in_proj)
    r_o = partner(readout_w)
    wh_o = partner(w_hidden)
    wo_o = partner(w_out)
    emb_o = partner(action_embed)
    ip = jnp.concatenate([in_proj, ip_o], axis=1)

    rates = jnp.concatenate(
        [
            lax.dynamic_slice_in_dim(decay_rates, m * half, half),
            lax.dynamic_slice_in_dim(decay_rates, (1 - m) * half, half),
        ]
    )
    decays = jnp.exp(-rates)
    scaling = jnp.sqrt(1.0 - decays * decays)
    width = decays.shape[0]

    seqs, steps, feat = inputs.shape
    bh = seqs // 2
    x = lax.dynamic_slice_in_dim(inputs, m * bh, bh, 0)
    driven = (
        jnp.dot(x.reshape(bh * steps, feat), ip, preferred_element_type=jnp.float32).reshape(
            bh, steps, width
        )
        * scaling
    )
    my_resets = lax.dynamic_slice_in_dim(resets, m * bh, bh, 0)
    keep = (1 - my_resets).astype(jnp.float32)
    sub = steps // ntm
    rows_sent = bh * sub
    lanes = -(-(2 * bh * width) // (rows_sent * 128)) * 128
    fused = sub % 16 == 0
    if fused:
        send_states, ends_local = scan_send(keep, decays, driven, ntm, lanes)
    else:
        local = local_scan(driven, keep[:, :, None] * decays)
        ends_local = local[:, -1, :]
        send_states = jnp.swapaxes(
            local.astype(jnp.bfloat16).reshape(bh, ntm, sub, width), 0, 1
        ).reshape(ntm, bh * sub, width)
    sub = steps // ntm
    positions = lax.broadcasted_iota(jnp.int32, my_resets.shape, 1)
    first = jnp.min(jnp.where(my_resets != 0, positions, steps), axis=1).astype(jnp.float32)

    ends_hi = ends_local.astype(jnp.bfloat16)
    ends_lo = (ends_local - ends_hi.astype(jnp.float32)).astype(jnp.bfloat16)
    room = rows_sent * lanes - bh * width - bh
    lo_flat = ends_lo.reshape(-1)[:room]
    extra = jnp.concatenate(
        [ends_hi.reshape(-1), first.astype(jnp.bfloat16), lo_flat]
    )
    extra = jnp.pad(extra, (0, rows_sent * lanes - extra.shape[0])).reshape(rows_sent, lanes)
    spread = jnp.broadcast_to(extra[None], (ntm,) + extra.shape)
    if fused:
        send = lax.dynamic_update_slice(send_states, spread, (0, 0, width))
    else:
        send = jnp.concatenate([send_states, spread], axis=2)
    got = lax.all_to_all(send, "tm", split_axis=0, concat_axis=0, tiled=True)
    recv = jnp.swapaxes(got[:, :, :width].reshape(ntm, bh, sub, width), 0, 1)
    flat = got[:, :, width:].reshape(ntm, -1)
    got_hi = flat[:, : bh * width].astype(jnp.float32)
    firsts = flat[:, bh * width : bh * width + bh].astype(jnp.float32)
    got_lo = flat[:, bh * width + bh : bh * width + bh + lo_flat.shape[0]].astype(jnp.float32)
    got_lo = jnp.pad(got_lo, ((0, 0), (0, bh * width - lo_flat.shape[0])))
    gathered = (got_hi + got_lo).reshape(ntm, bh, width)
    ends = gathered

    nblocks = gathered.shape[0]
    whole_block = decays ** steps
    gain = jnp.where(firsts >= steps, 1.0, 0.0)[:, :, None] * whole_block
    total = ends
    offset = 1
    while offset < nblocks:
        gain_prev = jnp.concatenate([jnp.ones_like(gain[:offset]), gain[:-offset]], axis=0)
        total_prev = jnp.concatenate([jnp.zeros_like(total[:offset]), total[:-offset]], axis=0)
        total = gain * total_prev + total
        gain = gain * gain_prev
        offset *= 2
    carry = jnp.concatenate([jnp.zeros_like(total[:1]), total[:-1]], axis=0)

    t_glob = d * sub + lax.broadcasted_iota(jnp.int32, (sub,), 0)
    powers = decays[None, :] ** (t_glob[:, None] + 1).astype(jnp.float32)
    alive = t_glob[None, None, :].astype(jnp.float32) < jnp.swapaxes(firsts, 0, 1)[:, :, None]
    cum = jnp.where(alive[..., None], powers[None, None], 0.0)
    posterior = recv.astype(jnp.float32) + cum * jnp.swapaxes(carry, 0, 1)[:, :, None, :]

    _, blocks, _, horizon = actions.shape
    rows = bh * blocks * sub
    current = posterior.reshape(rows, width)
    my_actions = lax.dynamic_slice_in_dim(actions, m * bh, bh, 0).reshape(rows, horizon)
    table = jnp.concatenate([action_embed, emb_o], axis=1)
    table = jnp.pad(table, ((0, 128 - table.shape[0]), (0, 0)))
    one_hot = (
        jnp.swapaxes(my_actions, 0, 1)[:, :, None] == jnp.arange(128, dtype=jnp.int32)
    ).astype(jnp.bfloat16)
    vecs = jnp.stack([decays, scaling, norm_gain], axis=0)
    side = jnp.reshape(m, (1,)).astype(jnp.int32)
    keep_part, give_part = imagine(
        side, current, one_hot, vecs, readout_w, r_o, w_hidden, wh_o, table, w_out, wo_o,
        in_proj, ip_o,
    )
    got = partner(give_part)

    def arrange(part):
        return jnp.transpose(part.reshape(horizon, bh, blocks, sub, half), (1, 2, 3, 0, 4))

    mine, theirs = arrange(keep_part), arrange(got)
    out = jnp.zeros((2 * bh,) + mine.shape[1:], mine.dtype)
    out = lax.dynamic_update_slice(out, mine, (m * bh, 0, 0, 0, 0))
    return lax.dynamic_update_slice(out, theirs, ((1 - m) * bh, 0, 0, 0, 0))


def _imagine_kernel(
    side_ref, cur_ref, hot_ref, vec_ref, r_a, r_b, wh_a, wh_b, emb_ref, wo_a, wo_b, ip_a, ip_b,
    keep_ref, give_ref,
):
    horizon, rows, _ = hot_ref.shape
    half = r_a.shape[0]
    width = 2 * half
    tile = 256
    lead = side_ref[0] == 0

    def dot(a, b):
        return jnp.dot(a, b, preferred_element_type=jnp.float32)

    def chunk(c, carry):
        rs = pl.ds(pl.multiple_of(c * tile, tile), tile)
        cur_a = cur_ref[rs, :half]
        cur_b = cur_ref[rs, half:]
        for step in range(horizon):
            f = dot(cur_a.astype(jnp.bfloat16), r_a[...]).astype(jnp.bfloat16).astype(
                jnp.float32
            ) + dot(cur_b.astype(jnp.bfloat16), r_b[...]).astype(jnp.bfloat16).astype(jnp.float32)
            mean_sq = jnp.sum(f * f, axis=-1, keepdims=True) * (1.0 / width)
            normed = (f * lax.rsqrt(mean_sq + 1e-06) * vec_ref[2:3, :]).astype(jnp.bfloat16)
            hot = hot_ref[step, rs, :]
            pre_a = dot(normed, wh_a[...]) + dot(hot, emb_ref[:, :half])
            pre_b = dot(normed, wh_b[...]) + dot(hot, emb_ref[:, half:])
            hid_a = (pre_a * jax.nn.sigmoid(pre_a)).astype(jnp.bfloat16)
            hid_b = (pre_b * jax.nn.sigmoid(pre_b)).astype(jnp.bfloat16)
            lo = (dot(hid_a, wo_a[:, :half]) + dot(hid_b, wo_b[:, :half])).astype(jnp.bfloat16)
            hi = (dot(hid_a, wo_a[:, half:]) + dot(hid_b, wo_b[:, half:])).astype(jnp.bfloat16)
            keep_ref[step, rs, :] = jnp.where(lead, lo, hi)
            give_ref[step, rs, :] = jnp.where(lead, hi, lo)
            if step < horizon - 1:
                up_a = dot(lo, ip_a[:half, :]) + dot(hi, ip_a[half:, :])
                up_b = dot(lo, ip_b[:half, :]) + dot(hi, ip_b[half:, :])
                cur_a = vec_ref[0:1, :half] * cur_a + vec_ref[1:2, :half] * up_a
                cur_b = vec_ref[0:1, half:] * cur_b + vec_ref[1:2, half:] * up_b
        return carry

    lax.fori_loop(0, rows // tile, chunk, 0)


def imagine(side, current, one_hot, vecs, *weights):
    horizon, rows, _ = one_hot.shape
    half = weights[0].shape[0]
    out = jax.ShapeDtypeStruct((horizon, rows, half), jnp.bfloat16)
    vmem = pl.BlockSpec(memory_space=pltpu.VMEM)
    flops = 2 * rows * horizon * 4 * (2 * half) * (2 * half)
    return pl.pallas_call(
        _imagine_kernel,
        out_shape=(out, out),
        in_specs=[pl.BlockSpec(memory_space=pltpu.SMEM)] + [vmem] * (3 + len(weights)),
        out_specs=(vmem, vmem),
        compiler_params=pltpu.CompilerParams(vmem_limit_bytes=48 * 1024 * 1024),
        cost_estimate=pl.CostEstimate(
            flops=flops, bytes_accessed=16 * 1024 * 1024, transcendentals=rows * horizon * 2 * half
        ),
    )(side, current, one_hot, vecs, *weights)


def solution(mesh):
    in_specs = (
        P("rep", "tm", None),
        P("rep", "tm"),
        P("rep", None, "tm", None),
        P(None, "mp"),
        P(),
        P("mp", None),
        P(),
        P(None, "mp"),
        P(None, "mp"),
        P("mp", None),
    )
    out_specs = P("rep", None, "tm", None, "mp")
    return jax.shard_map(
        per_device, mesh=mesh, in_specs=in_specs, out_specs=out_specs, check_vma=False
    )
```

profile of v0, /device:TPU:0, one launch (start us, length us, event | category | flops | bytes accessed | tf_op | source)
XLA Modules:
  0.0 56.5 jit_solution(12577760505744051581)
XLA Ops:
  0.0 0.0 copy-start
  0.0 0.5 collective-permute-start
  0.5 1.4 %fusion.14 = (s32[2]{0:T(128)S(1)}, f32[2,128]{1,0:T(2,128)}) fusion(s32[4,128]{1,0:T(4,128)} %param.11, s32[]{:T(128)S(6)} %select_n.27), kind=kLoop, calls=%fused_computation.49 | loop fusion | flops 1278 | bytes 2060 | tf_op jit(solution)/shard_map/reduce_min | solution.py:155
  1.9 0.8 %fusion.18 = (f32[512]{0:T(512)S(1)}, f32[512]{0:T(512)S(1)}) fusion(f32[1024]{0:T(1024)} %param.14, s32[]{:T(128)S(6)} %select_n.28, s32[]{:T(128)S(6)} %select_n.29), kind=kLoop, calls=%fused_computation.56 | loop fusion | bytes 8200 | tf_op jit(solution)/shard_map/dynamic_slice | solution.py:122
  2.7 0.6 %subtract_sqrt_fusion = (f32[1,1024]{1,0:T(1,128)S(1)}, f32[1,1024]{1,0:T(1,128)}) fusion(f32[1,512]{1,0:T(1,128)S(1)} %bitcast.65, f32[1,512]{1,0:T(1,128)S(1)} %bitcast.64), kind=kLoop, calls=%fused_computation.39 | loop fusion | flops 4096 | bytes 12288 | tf_op jit(solution)/shard_map/sqrt | solution.py:127
  3.3 0.0 collective-permute-done.ip_b
  3.4 0.0 copy-start.8
  3.4 1.0 %copy-done.8 = bf16[1024,512]{1,0:T(8,128)(2,1)} copy-done((bf16[1024,512]{1,0:T(8,128)(2,1)}, bf16[1024,512]{1,0:T(8,128)(2,1)S(1)}, u32[]{:S(2)}) %copy-start.8) | copy-done | bytes 1048600
  4.4 0.0 copy-done
  4.4 2.9 %fusion.3.x_ref = f32[2,128,1024]{2,1,0:T(8,128)} fusion(bf16[1024,512]{1,0:T(8,128)(2,1)S(1)} %collective-permute-done.ip_b, bf16[1024,512]{1,0:T(8,128)(2,1)} %ip_a.1, f32[1024]{0:T(1024)S(1)} %get-tuple-element.22, bf16[4,128,1024]{2,1,0:T(8,128)(2,1)S(1)} %copy-done, s32[]{:T(128)S(6)} %select_n.27), kind=kOutput, calls=%fused_computation.4 | convolution fusion | flops 541327360 | bytes 3674116 | tf_op jit(solution)/shard_map/dot_general | solution.py:134
  7.3 0.0 copy-start.7
  7.3 2.8 %shard_map.100 = (bf16[8,32,1152]{2,1,0:T(8,128)(2,1)}, f32[2,1024]{1,0:T(2,128)}) custom-call(f32[2,128]{1,0:T(2,128)} %get-tuple-element.27.keep_ref, f32[1,1024]{1,0:T(1,128)} %get-tuple-element.14.dec_ref, f32[2,128,1024]{2,1,0:T(8,128)} %fusion.3.x_ref), custom_call_target="tpu_custom_call" | custom-call | flops 786432 | bytes 1572864 | tf_op jit(solution)/shard_map/pallas_call | solution.py:66
  10.1 0.8 %fusion.9 = (bf16[1,8,2,128]{3,2,1,0:T(2,128)(2,1)S(1)}, bf16[1,8,2,128]{3,2,1,0:T(2,128)(2,1)S(1)}) fusion(f32[2,1024]{1,0:T(2,128)} %get-tuple-element.10), kind=kLoop, calls=%fused_computation.32 | loop fusion | flops 8192 | bytes 16384
  10.9 0.1 concatenate.60
  11.0 0.7 %broadcast_dynamic-update-slice_fusion = bf16[8,32,1152]{2,1,0:T(8,128)(2,1)} fusion(bf16[8,32,1152]{2,1,0:T(8,128)(2,1)} %get-tuple-element.9, bf16[32,128]{1,0:T(8,128)(2,1)S(1)} %bitcast.63), kind=kLoop, calls=%fused_computation.27 | loop fusion | bytes 73728 | tf_op jit(solution)/shard_map/dynamic_update_slice | solution.py:167
  11.7 6.9 %all-to-all-start = ((bf16[8,32,1152]{2,1,0:T(8,128)(2,1)}), bf16[8,32,1152]{2,1,0:T(8,128)(2,1)S(1)}, u32[]{:S(2)}, u32[]{:S(2)}) async-start(bf16[8,32,1152]{2,1,0:T(8,128)(2,1)} %broadcast_dynamic-update-slice_fusion), calls=%async_computation | async-start | bytes 1179648 | tf_op jit(solution)/shard_map/all_to_all | solution.py:170
  18.6 0.0 copy-done.5
  18.6 0.2 collective-permute-start.3
  18.8 0.0 copy-done.1
  18.8 0.4 collective-permute-start.1
  19.2 0.1 collective-permute-start.2
  19.3 0.4 collective-permute-start.4
  19.7 0.1 reshape.176
  19.8 0.1 broadcast_power_fusion
  20.0 0.2 fusion.7.hot_ref
  20.2 0.0 collective-permute-done.3
  20.2 14.8 %all-to-all-done = bf16[8,32,1152]{2,1,0:T(8,128)(2,1)S(1)} async-done(((bf16[8,32,1152]{2,1,0:T(8,128)(2,1)}), bf16[8,32,1152]{2,1,0:T(8,128)(2,1)S(1)}, u32[]{:S(2)}, u32[]{:S(2)}) %all-to-all-start) | async-done | bytes 589856 | tf_op jit(solution)/shard_map/all_to_all | solution.py:170
  35.1 0.1 slice.59
  35.2 0.1 copy.19
  35.3 0.1 copy.18
  35.4 0.1 broadcast_multiply_fusion
  35.5 0.1 multiply_add_fusion
  35.6 0.1 slice.53
  35.7 0.1 broadcast_compare_fusion
  35.8 0.2 bitcast_add_fusion
  36.0 0.0 collective-permute-done.1.r_b
  36.0 0.0 collective-permute-done.2.wh_b
  36.0 0.0 collective-permute-done.4.wo_b
  36.0 0.0 copy-start.2
  36.1 1.2 %copy-done.2 = bf16[512,1024]{1,0:T(8,128)(2,1)S(1)} copy-done((bf16[512,1024]{1,0:T(8,128)(2,1)S(1)}, bf16[512,1024]{1,0:T(8,128)(2,1)}, u32[]{:S(2)}) %copy-start.2) | copy-done | bytes 1048600
  37.3 14.2 %shard_map.101 = (bf16[4,256,512]{2,1,0:T(8,128)(2,1)S(1)}, bf16[4,256,512]{2,1,0:T(8,128)(2,1)}) custom-call(s32[1]{0:T(128)} %bitcast.side_ref, f32[256,1024]{1,0:T(8,128)S(1)} %bitcast.51, bf16[4,256,128]{2,1,0:T(8,128)(2,1)S(1)} %fusion.7.hot_ref, f32[3,1024]{1,0:T(4,128)S(1)} %pad_maximum_fusion.vec_ref, bf16[512,1024]{1,0:T(8,128)(2,1)S(1)} %copy-done.2, ...), custom_call_target="tpu_custom_call" | custom-call | flops 8589934592 | bytes 16777216 | tf_op jit(solution)/shard_map/pallas_call | solution.py:273
  51.5 0.0 collective-permute-start.5
  51.5 0.9 %broadcast_in_dim.38 = bf16[4,8,16,4,512]{4,3,2,1,0:T(4,128)(2,1)S(1)} broadcast(bf16[]{:T(256)} %constant.15.clone.1), dimensions={} | broadcast | bytes 2097154 | tf_op jit(solution)/shard_map/broadcast_in_dim | solution.py:220
  52.4 0.9 %bitcast_dynamic-update-slice_fusion.1 = bf16[4,8,16,4,512]{4,3,2,1,0:T(4,128)(2,1)S(1)} fusion(bf16[4,8,16,4,512]{4,3,2,1,0:T(4,128)(2,1)S(1)} %broadcast_in_dim.38, s32[]{:T(128)S(6)} %select_n.27, bf16[4,2,8,16,512]{4,3,2,1,0:T(8,128)(2,1)S(1)} %bitcast.50), kind=kLoop, calls=%fused_computation.6 | loop fusion | bytes 2097156 | tf_op jit(solution)/shard_map/dynamic_update_slice | solution.py:221
  53.4 0.0 copy-start.3
  53.4 1.0 %collective-permute-done.5 = bf16[4,256,512]{2,1,0:T(8,128)(2,1)S(1)} collective-permute-done((bf16[4,256,512]{2,1,0:T(8,128)(2,1)}, bf16[4,256,512]{2,1,0:T(8,128)(2,1)S(1)}, u32[]{:S(2)}, u32[]{:S(2)}) %collective-permute-start.5) | collective-permute-done | bytes 1048608 | tf_op jit(solution)/shard_map/ppermute | solution.py:110
  54.4 0.3 copy-done.3
  54.7 1.8 %bitcast_dynamic-update-slice_fusion = bf16[4,8,16,4,512]{4,3,2,1,0:T(4,128)(2,1)} fusion(bf16[4,8,16,4,512]{4,3,2,1,0:T(4,128)(2,1)} %copy-done.3, s32[]{:T(128)S(6)} %select_n.33, bf16[4,2,8,16,512]{4,3,2,1,0:T(8,128)(2,1)S(1)} %bitcast.53), kind=kLoop, calls=%fused_computation.5 | loop fusion | bytes 2097156 | tf_op jit(solution)/shard_map/dynamic_update_slice | solution.py:222
  (23 shorter events, 0.2 us)
Async XLA Ops:
  0.0 4.4 %copy-start = (bf16[4,128,1024]{2,1,0:T(8,128)(2,1)S(1)}, bf16[4,128,1024]{2,1,0:T(8,128)(2,1)}, u32[]{:S(2)}) copy-start(bf16[4,128,1024]{2,1,0:T(8,128)(2,1)} %param.10) | copy-start | bytes 3145732
  0.0 3.3 %collective-permute-start = (bf16[1024,512]{1,0:T(8,128)(2,1)}, bf16[1024,512]{1,0:T(8,128)(2,1)S(1)}, u32[]{:S(2)}, u32[]{:S(2)}) collective-permute-start(bf16[1024,512]{1,0:T(8,128)(2,1)} %ip_a.1), channel_id=1, source_target_pairs={{0,1},{1,0},{2,3},{3,2},{4,5},{5,4},{6,7},{7,6},{8,9},{9,8},{10,11... | collective-permute-start | bytes 3145736 | tf_op jit(solution)/shard_map/ppermute | solution.py:110
  3.4 1.0 %copy-start.8 = (bf16[1024,512]{1,0:T(8,128)(2,1)}, bf16[1024,512]{1,0:T(8,128)(2,1)S(1)}, u32[]{:S(2)}) copy-start(bf16[1024,512]{1,0:T(8,128)(2,1)S(1)} %collective-permute-done.ip_b) | copy-start | bytes 3145732
  7.3 11.3 %copy-start.5 = (bf16[18,512]{1,0:T(8,128)(2,1)S(1)}, bf16[18,512]{1,0:T(8,128)(2,1)}, u32[]{:S(2)}) copy-start(bf16[18,512]{1,0:T(8,128)(2,1)} %param.18) | copy-start | bytes 55300
  7.3 11.5 %copy-start.1 = (bf16[512,1024]{1,0:T(8,128)(2,1)S(1)}, bf16[512,1024]{1,0:T(8,128)(2,1)}, u32[]{:S(2)}) copy-start(bf16[512,1024]{1,0:T(8,128)(2,1)} %r_a.1) | copy-start | bytes 3145732
  7.3 12.4 %copy-start.6 = (s32[4,8,16,4]{2,3,1,0:T(4,128)S(1)}, s32[4,8,16,4]{2,3,1,0:T(4,128)}, u32[]{:S(2)}) copy-start(s32[4,8,16,4]{2,3,1,0:T(4,128)} %param.12) | copy-start | bytes 24580
  7.3 12.9 %copy-start.4 = (f32[1,1024]{1,0:T(1,128)S(1)}, f32[1,1024]{1,0:T(1,128)}, u32[]{:S(2)}) copy-start(f32[1,1024]{1,0:T(1,128)} %get-tuple-element.14.dec_ref) | copy-start | bytes 12292
  7.3 12.9 %copy-start.7 = (f32[1024]{0:T(1024)S(1)}, f32[1024]{0:T(1024)}, u32[]{:S(2)}) copy-start(f32[1024]{0:T(1024)} %param.16) | copy-start | bytes 12292
  11.7 23.4 %all-to-all-start = ((bf16[8,32,1152]{2,1,0:T(8,128)(2,1)}), bf16[8,32,1152]{2,1,0:T(8,128)(2,1)S(1)}, u32[]{:S(2)}, u32[]{:S(2)}) async-start(bf16[8,32,1152]{2,1,0:T(8,128)(2,1)} %broadcast_dynamic-update-slice_fusion), calls=%async_computation | async-start | bytes 1179648 | tf_op jit(solution)/shard_map/all_to_all | solution.py:170
  18.6 1.6 %collective-permute-start.3 = (bf16[18,512]{1,0:T(8,128)(2,1)S(1)}, bf16[18,512]{1,0:T(8,128)(2,1)S(1)}, u32[]{:S(2)}, u32[]{:S(2)}) collective-permute-start(bf16[18,512]{1,0:T(8,128)(2,1)S(1)} %copy-done.5), channel_id=1, source_target_pairs={{0,1},{1,0},{2,3},{3,2},{4,5},{5,4},{6,7},{7,6},{8,9},{9,8},{10,11... | collective-permute-start | bytes 55304 | tf_op jit(solution)/shard_map/ppermute | solution.py:110
  18.8 17.2 %collective-permute-start.1 = (bf16[512,1024]{1,0:T(8,128)(2,1)S(1)}, bf16[512,1024]{1,0:T(8,128)(2,1)}, u32[]{:S(2)}, u32[]{:S(2)}) collective-permute-start(bf16[512,1024]{1,0:T(8,128)(2,1)S(1)} %copy-done.1), channel_id=1, source_target_pairs={{0,1},{1,0},{2,3},{3,2},{4,5},{5,4},{6,7},{7,6},{8,9},{9,8},{10,11... | collective-permute-start | bytes 3145736 | tf_op jit(solution)/shard_map/ppermute | solution.py:110
  19.2 16.8 %collective-permute-start.2 = (bf16[1024,512]{1,0:T(8,128)(2,1)}, bf16[1024,512]{1,0:T(8,128)(2,1)}, u32[]{:S(2)}, u32[]{:S(2)}) collective-permute-start(bf16[1024,512]{1,0:T(8,128)(2,1)} %wh_a.1), channel_id=1, source_target_pairs={{0,1},{1,0},{2,3},{3,2},{4,5},{5,4},{6,7},{7,6},{8,9},{9,8},{10,11... | collective-permute-start | bytes 3145736 | tf_op jit(solution)/shard_map/ppermute | solution.py:110
  19.3 16.7 %collective-permute-start.4 = (bf16[512,1024]{1,0:T(8,128)(2,1)}, bf16[512,1024]{1,0:T(8,128)(2,1)}, u32[]{:S(2)}, u32[]{:S(2)}) collective-permute-start(bf16[512,1024]{1,0:T(8,128)(2,1)} %wo_a.1), channel_id=1, source_target_pairs={{0,1},{1,0},{2,3},{3,2},{4,5},{5,4},{6,7},{7,6},{8,9},{9,8},{10,11... | collective-permute-start | bytes 3145736 | tf_op jit(solution)/shard_map/ppermute | solution.py:110
  36.0 1.2 %copy-start.2 = (bf16[512,1024]{1,0:T(8,128)(2,1)S(1)}, bf16[512,1024]{1,0:T(8,128)(2,1)}, u32[]{:S(2)}) copy-start(bf16[512,1024]{1,0:T(8,128)(2,1)} %r_a.1) | copy-start | bytes 3145732
  51.5 2.9 %collective-permute-start.5 = (bf16[4,256,512]{2,1,0:T(8,128)(2,1)}, bf16[4,256,512]{2,1,0:T(8,128)(2,1)S(1)}, u32[]{:S(2)}, u32[]{:S(2)}) collective-permute-start(bf16[4,256,512]{2,1,0:T(8,128)(2,1)} %get-tuple-element.12), channel_id=1, source_target_pairs={{0,1},{1,0},{2,3},{3,2},{4,5},{5,4},{6,7},{7,6},{8,9},{9,8},{10,11... | collective-permute-start | bytes 3145736 | tf_op jit(solution)/shard_map/ppermute | solution.py:110
  53.4 1.3 %copy-start.3 = (bf16[4,8,16,4,512]{4,3,2,1,0:T(4,128)(2,1)}, bf16[4,8,16,4,512]{4,3,2,1,0:T(4,128)(2,1)S(1)}, u32[]{:S(2)}) copy-start(bf16[4,8,16,4,512]{4,3,2,1,0:T(4,128)(2,1)S(1)} %bitcast_dynamic-update-slice_fusion.1) | copy-start | bytes 6291460
where the time goes:
time: 56.9 us; the launch traced here: 56.5 us
  Pallas kernels  17.1 us (30%)
  waiting for transfers between devices  15.8 us (28%)
  local copies, waits for them, and re-layouts  8.51 us (15%)
  starting transfers between devices  8.5 us (15%)
  other arithmetic  3.53 us (6%)
  matrix products  2.91 us (5%)
    all_to_all x1, waiting for transfers between devices, per_device(): got = lax.all_to_all(send, 'tm', split_axis=0, concat_axis=0, tiled=True)  14.8 us
    pallas_call x1, Pallas kernels, imagine(): pl.pallas_call(_imagine_kernel, out_shape=(out, out), in_specs=[pl.BlockS...  14.2 us
    all_to_all x1, starting transfers between devices, per_device(): got = lax.all_to_all(send, 'tm', split_axis=0, concat_axis=0, tiled=True)  6.92 us
    dot_general x1, matrix products, per_device(): jnp.dot(x.reshape(bh * steps, feat), ip, preferred_element_type=jnp.float32)  2.91 us
    pallas_call x1, Pallas kernels, scan_send(): pl.pallas_call(_scan_send_kernel, out_shape=(jax.ShapeDtypeStruct((ntm, n...  2.83 us
    unnamed x20, local copies, waits for them, and re-layouts  2.62 us
    dynamic_update_slice x1, local copies, waits for them, and re-layouts, per_device(): return lax.dynamic_update_slice(out, theirs, ((1 - m) * bh, 0, 0, 0, 0))  1.84 us
    ppermute x6, starting transfers between devices, partner(): return lax.ppermute(x, 'mp', swap)  1.58 us
  transfers between devices with their start and end apart: 7, of which 2 were waited for; matrix products, arithmetic and copies ran while one was open for 11% of the time, Pallas kernels for 0%

commit v1 on v0

--- a/solution.py
+++ b/solution.py
@@ -33,35 +33,42 @@
     )(driven, gates)
 
 
-def _scan_send_kernel(keep_ref, dec_ref, x_ref, send_ref, ends_ref, buf):
-    nb, steps, width = x_ref.shape
+def _scan_send_kernel(keep_ref, dec_ref, xa_ref, xb_ref, send_ref, ends_ref, buf):
+    nb, steps, half = xa_ref.shape
+    width = 2 * half
     ntm, rows_sent, _ = send_ref.shape
     sub = rows_sent // nb
-    dec = dec_ref[...]
+    dec_a = dec_ref[:, :half]
+    dec_b = dec_ref[:, half:]
 
     def body(t, states):
         row = pl.ds(t, 1)
         new = []
         for b in range(nb):
-            h = (keep_ref[b, t] * dec) * states[b] + x_ref[b, row, :]
-            buf[b, row, :] = h
-            new.append(h)
+            keep_now = keep_ref[b, t]
+            ha = (keep_now * dec_a) * states[2 * b] + xa_ref[b, row, :]
+            hb = (keep_now * dec_b) * states[2 * b + 1] + xb_ref[b, row, :]
+            buf[b, row, pl.ds(0, half)] = ha
+            buf[b, row, pl.ds(half, half)] = hb
+            new += [ha, hb]
         return tuple(new)
 
-    start = tuple(jnp.zeros((1, width), jnp.float32) for _ in range(nb))
+    start = tuple(jnp.zeros((1, half), jnp.float32) for _ in range(2 * nb))
     final = lax.fori_loop(0, steps, body, start, unroll=8)
     for b in range(nb):
-        ends_ref[pl.ds(b, 1), :] = final[b]
+        ends_ref[pl.ds(b, 1), pl.ds(0, half)] = final[2 * b]
+        ends_ref[pl.ds(b, 1), pl.ds(half, half)] = final[2 * b + 1]
         for j in range(ntm):
             send_ref[j, pl.ds(b * sub, sub), pl.ds(0, width)] = buf[b, pl.ds(j * sub, sub), :].astype(
                 jnp.bfloat16
             )
 
 
-def scan_send(keep, decays, driven, ntm, spare):
-    nb, steps, width = driven.shape
+def scan_send(keep, decays, driven_a, driven_b, ntm, spare):
+    nb, steps, half = driven_a.shape
+    width = 2 * half
     sub = steps // ntm
-    size = driven.size
+    size = 2 * driven_a.size
     vmem = pl.BlockSpec(memory_space=pltpu.VMEM)
     return pl.pallas_call(
         _scan_send_kernel,
@@ -69,11 +76,11 @@
             jax.ShapeDtypeStruct((ntm, nb * sub, width + spare), jnp.bfloat16),
             jax.ShapeDtypeStruct((nb, width), jnp.float32),
         ),
-        in_specs=[pl.BlockSpec(memory_space=pltpu.SMEM), vmem, vmem],
+        in_specs=[pl.BlockSpec(memory_space=pltpu.SMEM), vmem, vmem, vmem],
         out_specs=(vmem, vmem),
         scratch_shapes=[pltpu.VMEM((nb, steps, width), jnp.float32)],
         cost_estimate=pl.CostEstimate(flops=3 * size, bytes_accessed=6 * size, transcendentals=0),
-    )(keep, decays.reshape(1, width), driven)
+    )(keep, decays.reshape(1, width), driven_a, driven_b)
 
 
 def gather_blocks(value, axis, mine, count):
@@ -143,7 +150,14 @@
     lanes = -(-(2 * bh * width) // (rows_sent * 128)) * 128
     fused = sub % 16 == 0
     if fused:
-        send_states, ends_local = scan_send(keep, decays, driven, ntm, lanes)
+        flat_x = x.reshape(bh * steps, feat)
+        driven_a = jnp.dot(flat_x, in_proj, preferred_element_type=jnp.float32).reshape(
+            bh, steps, half
+        ) * scaling[:half]
+        driven_b = jnp.dot(flat_x, ip_o, preferred_element_type=jnp.float32).reshape(
+            bh, steps, half
+        ) * scaling[half:]
+        send_states, ends_local = scan_send(keep, decays, driven_a, driven_b, ntm, lanes)
     else:
         local = local_scan(driven, keep[:, :, None] * decays)
         ends_local = local[:, -1, :]

time: 56.9 us -> 56.8 us (level)
  local copies, waits for them, and re-layouts: 8.51 us -> 7.5 us
  matrix products: 2.91 us -> 3.72 us
    unnamed x20, local copies, waits for them, and re-layouts: 2.62 us -> 1.64 us
    dot_general x1 -> x2, matrix products: 2.91 us -> 3.72 us  [the longest x1 2.47 us: per_device(): jnp.dot(flat_x, in_proj, preferred_element_type=jnp.float32)]
  transfers between devices with their start and end apart: 7 -> 7, of which waited for: 2 -> 2; matrix products, arithmetic and copies ran while one was open for 11% -> 15% of each run, Pallas kernels for 0% -> 0%
where the time goes in v1:
time: 56.8 us; the launch traced here: 56.5 us
  Pallas kernels  17.2 us (30%)
  waiting for transfers between devices  15.9 us (28%)
  starting transfers between devices  8.44 us (15%)
  local copies, waits for them, and re-layouts  7.5 us (13%)
  matrix products  3.72 us (7%)
  other arithmetic  3.52 us (6%)
    all_to_all x1, waiting for transfers between devices, per_device(): got = lax.all_to_all(send, 'tm', split_axis=0, concat_axis=0, tiled=True)  14.9 us
    pallas_call x1, Pallas kernels, imagine(): pl.pallas_call(_imagine_kernel, out_shape=(out, out), in_specs=[pl.BlockS...  14.2 us
    all_to_all x1, starting transfers between devices, per_device(): got = lax.all_to_all(send, 'tm', split_axis=0, concat_axis=0, tiled=True)  6.86 us
    pallas_call x1, Pallas kernels, scan_send(): pl.pallas_call(_scan_send_kernel, out_shape=(jax.ShapeDtypeStruct((ntm, n...  2.97 us
    dot_general x1, matrix products, per_device(): jnp.dot(flat_x, in_proj, preferred_element_type=jnp.float32)  2.47 us
    dynamic_update_slice x1, local copies, waits for them, and re-layouts, per_device(): return lax.dynamic_update_slice(out, theirs, ((1 - m) * bh, 0, 0, 0, 0))  1.84 us
    unnamed x20, local copies, waits for them, and re-layouts  1.64 us
    ppermute x6, starting transfers between devices, partner(): return lax.ppermute(x, 'mp', swap)  1.58 us
  transfers between devices with their start and end apart: 7, of which 2 were waited for; matrix products, arithmetic and copies ran while one was open for 15% of the time, Pallas kernels for 0%

profile of v1, /device:TPU:0, one launch (start us, length us, event | category | flops | bytes accessed | tf_op | source)
XLA Modules:
  0.0 56.5 jit_solution(2124552130107640086)
XLA Ops:
  0.0 0.0 copy-start
  0.0 0.5 collective-permute-start
  0.5 0.8 %fusion.18 = (f32[512]{0:T(512)S(1)}, f32[512]{0:T(512)S(1)}) fusion(f32[1024]{0:T(1024)} %param.14, s32[]{:T(128)S(6)} %select_n.28, s32[]{:T(128)S(6)} %select_n.29), kind=kLoop, calls=%fused_computation.57 | loop fusion | bytes 8200 | tf_op jit(solution)/shard_map/dynamic_slice | solution.py:129
  1.3 1.4 %fusion.14 = (s32[2]{0:T(128)S(1)}, f32[2,128]{1,0:T(2,128)}) fusion(s32[4,128]{1,0:T(4,128)} %param.11, s32[]{:T(128)S(6)} %select_n.27), kind=kLoop, calls=%fused_computation.50 | loop fusion | flops 1278 | bytes 2060 | tf_op jit(solution)/shard_map/reduce_min | solution.py:169
  2.7 0.6 %subtract_sqrt_fusion = (f32[1,1024]{1,0:T(1,128)S(1)}, f32[1,1024]{1,0:T(1,128)}) fusion(f32[1,512]{1,0:T(1,128)S(1)} %bitcast.66, f32[1,512]{1,0:T(1,128)S(1)} %bitcast.65), kind=kLoop, calls=%fused_computation.39 | loop fusion | flops 4096 | bytes 12288 | tf_op jit(solution)/shard_map/sqrt | solution.py:134
  3.3 0.0 copy-done
  3.4 2.5 %convolution_multiply_fusion.1.xa_ref = f32[2,128,512]{2,1,0:T(8,128)} fusion(bf16[1024,512]{1,0:T(8,128)(2,1)} %ip_a.1, bf16[4,128,1024]{2,1,0:T(8,128)(2,1)S(1)} %copy-done, s32[]{:T(128)S(6)} %select_n.27, f32[512]{0:T(512)S(1)} %get-tuple-element.25), kind=kOutput, calls=%fused_computation.1 | convolution fusion | flops 268566528 | bytes 2099204 | tf_op jit(solution)/shard_map/dot_general | solution.py:154
  5.8 0.0 collective-permute-done.ip_b
  5.8 0.0 copy-start.7
  5.8 0.0 copy-start.5
  5.9 0.0 copy-start.8
  5.9 1.2 %convolution_multiply_fusion.xb_ref = f32[2,128,512]{2,1,0:T(8,128)} fusion(bf16[1024,512]{1,0:T(8,128)(2,1)S(1)} %collective-permute-done.ip_b, bf16[4,128,1024]{2,1,0:T(8,128)(2,1)S(1)} %copy-done, s32[]{:T(128)S(6)} %select_n.27, f32[512]{0:T(512)S(1)} %get-tuple-element.24), kind=kOutput, calls=%fused_computation | convolution fusion | flops 268566528 | bytes 2099204 | tf_op jit(solution)/shard_map/dot_general | solution.py:157
  7.1 3.0 %shard_map.100 = (bf16[8,32,1152]{2,1,0:T(8,128)(2,1)}, f32[2,1024]{1,0:T(2,128)}) custom-call(f32[2,128]{1,0:T(2,128)} %get-tuple-element.29.keep_ref, f32[1,1024]{1,0:T(1,128)} %get-tuple-element.14.dec_ref, f32[2,128,512]{2,1,0:T(8,128)} %convolution_multiply_fusion.1.xa_ref, f32[2,128,512]{2,1,0:T(8,128)} %convolution_multiply_fusion.xb_ref), custom_call_target="tpu_custom_call" | custom-call | flops 786432 | bytes 1572864 | tf_op jit(solution)/shard_map/pallas_call | solution.py:73
  10.1 0.8 %fusion.8 = (bf16[1,8,2,128]{3,2,1,0:T(2,128)(2,1)S(1)}, bf16[1,8,2,128]{3,2,1,0:T(2,128)(2,1)S(1)}) fusion(f32[2,1024]{1,0:T(2,128)} %get-tuple-element.10), kind=kLoop, calls=%fused_computation.32 | loop fusion | flops 8192 | bytes 16384
  10.9 0.1 concatenate.53
  11.0 0.7 %broadcast_dynamic-update-slice_fusion = bf16[8,32,1152]{2,1,0:T(8,128)(2,1)} fusion(bf16[8,32,1152]{2,1,0:T(8,128)(2,1)} %get-tuple-element.9, bf16[32,128]{1,0:T(8,128)(2,1)S(1)} %bitcast.64), kind=kLoop, calls=%fused_computation.27 | loop fusion | bytes 73728 | tf_op jit(solution)/shard_map/dynamic_update_slice | solution.py:181
  11.6 6.9 %all-to-all-start = ((bf16[8,32,1152]{2,1,0:T(8,128)(2,1)}), bf16[8,32,1152]{2,1,0:T(8,128)(2,1)S(1)}, u32[]{:S(2)}, u32[]{:S(2)}) async-start(bf16[8,32,1152]{2,1,0:T(8,128)(2,1)} %broadcast_dynamic-update-slice_fusion), calls=%async_computation | async-start | bytes 1179648 | tf_op jit(solution)/shard_map/all_to_all | solution.py:184
  18.5 0.0 copy-done.6
  18.5 0.2 collective-permute-start.3
  18.8 0.3 collective-permute-start.1
  19.1 0.2 collective-permute-start.2
  19.3 0.3 collective-permute-start.4
  19.6 0.1 reshape.171
  19.7 0.1 broadcast_power_fusion
  19.8 0.2 fusion.4.hot_ref
  20.1 0.0 collective-permute-done.3
  20.1 14.9 %all-to-all-done = bf16[8,32,1152]{2,1,0:T(8,128)(2,1)S(1)} async-done(((bf16[8,32,1152]{2,1,0:T(8,128)(2,1)}), bf16[8,32,1152]{2,1,0:T(8,128)(2,1)S(1)}, u32[]{:S(2)}, u32[]{:S(2)}) %all-to-all-start) | async-done | bytes 589856 | tf_op jit(solution)/shard_map/all_to_all | solution.py:184
  35.1 0.1 slice.67
  35.2 0.1 copy.19
  35.2 0.1 copy.18
  35.3 0.1 broadcast_multiply_fusion
  35.4 0.1 multiply_add_fusion
  35.5 0.1 slice.61
  35.7 0.1 broadcast_compare_fusion
  35.7 0.2 bitcast_add_fusion
  36.0 0.0 collective-permute-done.1.r_b
  36.0 0.0 collective-permute-done.2.wh_b
  36.0 0.0 collective-permute-done.4.wo_b
  36.0 0.0 copy-start.2
  36.0 1.2 %copy-done.2 = bf16[512,1024]{1,0:T(8,128)(2,1)S(1)} copy-done((bf16[512,1024]{1,0:T(8,128)(2,1)S(1)}, bf16[512,1024]{1,0:T(8,128)(2,1)}, u32[]{:S(2)}) %copy-start.2) | copy-done | bytes 1048600
  37.2 14.2 %shard_map.101 = (bf16[4,256,512]{2,1,0:T(8,128)(2,1)S(1)}, bf16[4,256,512]{2,1,0:T(8,128)(2,1)}) custom-call(s32[1]{0:T(128)} %bitcast.side_ref, f32[256,1024]{1,0:T(8,128)S(1)} %bitcast.52, bf16[4,256,128]{2,1,0:T(8,128)(2,1)S(1)} %fusion.4.hot_ref, f32[3,1024]{1,0:T(4,128)S(1)} %pad_maximum_fusion.vec_ref, bf16[512,1024]{1,0:T(8,128)(2,1)S(1)} %copy-done.2, ...), custom_call_target="tpu_custom_call" | custom-call | flops 8589934592 | bytes 16777216 | tf_op jit(solution)/shard_map/pallas_call | solution.py:287
  51.4 0.0 collective-permute-start.5
  51.4 0.9 %broadcast_in_dim.38 = bf16[4,8,16,4,512]{4,3,2,1,0:T(4,128)(2,1)S(1)} broadcast(bf16[]{:T(256)} %constant.15.clone.1), dimensions={} | broadcast | bytes 2097154 | tf_op jit(solution)/shard_map/broadcast_in_dim | solution.py:234
  52.3 0.9 %bitcast_dynamic-update-slice_fusion.1 = bf16[4,8,16,4,512]{4,3,2,1,0:T(4,128)(2,1)S(1)} fusion(bf16[4,8,16,4,512]{4,3,2,1,0:T(4,128)(2,1)S(1)} %broadcast_in_dim.38, s32[]{:T(128)S(6)} %select_n.27, bf16[4,2,8,16,512]{4,3,2,1,0:T(8,128)(2,1)S(1)} %bitcast.51), kind=kLoop, calls=%fused_computation.3 | loop fusion | bytes 2097156 | tf_op jit(solution)/shard_map/dynamic_update_slice | solution.py:235
  53.3 0.0 copy-start.3
  53.3 1.0 %collective-permute-done.5 = bf16[4,256,512]{2,1,0:T(8,128)(2,1)S(1)} collective-permute-done((bf16[4,256,512]{2,1,0:T(8,128)(2,1)}, bf16[4,256,512]{2,1,0:T(8,128)(2,1)S(1)}, u32[]{:S(2)}, u32[]{:S(2)}) %collective-permute-start.5) | collective-permute-done | bytes 1048608 | tf_op jit(solution)/shard_map/ppermute | solution.py:117
  54.3 0.3 copy-done.3
  54.6 1.8 %bitcast_dynamic-update-slice_fusion = bf16[4,8,16,4,512]{4,3,2,1,0:T(4,128)(2,1)} fusion(bf16[4,8,16,4,512]{4,3,2,1,0:T(4,128)(2,1)} %copy-done.3, s32[]{:T(128)S(6)} %select_n.33, bf16[4,2,8,16,512]{4,3,2,1,0:T(8,128)(2,1)S(1)} %bitcast.54), kind=kLoop, calls=%fused_computation.2 | loop fusion | bytes 2097156 | tf_op jit(solution)/shard_map/dynamic_update_slice | solution.py:236
  (25 shorter events, 0.2 us)
Async XLA Ops:
  0.0 3.3 %copy-start = (bf16[4,128,1024]{2,1,0:T(8,128)(2,1)S(1)}, bf16[4,128,1024]{2,1,0:T(8,128)(2,1)}, u32[]{:S(2)}) copy-start(bf16[4,128,1024]{2,1,0:T(8,128)(2,1)} %param.10) | copy-start | bytes 3145732
  0.0 5.8 %collective-permute-start = (bf16[1024,512]{1,0:T(8,128)(2,1)}, bf16[1024,512]{1,0:T(8,128)(2,1)S(1)}, u32[]{:S(2)}, u32[]{:S(2)}) collective-permute-start(bf16[1024,512]{1,0:T(8,128)(2,1)} %ip_a.1), channel_id=1, source_target_pairs={{0,1},{1,0},{2,3},{3,2},{4,5},{5,4},{6,7},{7,6},{8,9},{9,8},{10,11... | collective-permute-start | bytes 3145736 | tf_op jit(solution)/shard_map/ppermute | solution.py:117
  5.8 5.8 %copy-start.4 = (bf16[1024,512]{1,0:T(8,128)(2,1)}, bf16[1024,512]{1,0:T(8,128)(2,1)S(1)}, u32[]{:S(2)}) copy-start(bf16[1024,512]{1,0:T(8,128)(2,1)S(1)} %collective-permute-done.ip_b) | copy-start | bytes 3145732
  5.8 12.7 %copy-start.6 = (bf16[18,512]{1,0:T(8,128)(2,1)S(1)}, bf16[18,512]{1,0:T(8,128)(2,1)}, u32[]{:S(2)}) copy-start(bf16[18,512]{1,0:T(8,128)(2,1)} %param.18) | copy-start | bytes 55300
  5.8 12.9 %copy-start.1 = (bf16[512,1024]{1,0:T(8,128)(2,1)S(1)}, bf16[512,1024]{1,0:T(8,128)(2,1)}, u32[]{:S(2)}) copy-start(bf16[512,1024]{1,0:T(8,128)(2,1)} %r_a.1) | copy-start | bytes 3145732
  5.8 13.8 %copy-start.7 = (s32[4,8,16,4]{2,3,1,0:T(4,128)S(1)}, s32[4,8,16,4]{2,3,1,0:T(4,128)}, u32[]{:S(2)}) copy-start(s32[4,8,16,4]{2,3,1,0:T(4,128)} %param.12) | copy-start | bytes 24580
  5.8 14.2 %copy-start.5 = (f32[1,1024]{1,0:T(1,128)S(1)}, f32[1,1024]{1,0:T(1,128)}, u32[]{:S(2)}) copy-start(f32[1,1024]{1,0:T(1,128)} %get-tuple-element.14.dec_ref) | copy-start | bytes 12292
  5.9 14.2 %copy-start.8 = (f32[1024]{0:T(1024)S(1)}, f32[1024]{0:T(1024)}, u32[]{:S(2)}) copy-start(f32[1024]{0:T(1024)} %param.16) | copy-start | bytes 12292
  11.6 23.4 %all-to-all-start = ((bf16[8,32,1152]{2,1,0:T(8,128)(2,1)}), bf16[8,32,1152]{2,1,0:T(8,128)(2,1)S(1)}, u32[]{:S(2)}, u32[]{:S(2)}) async-start(bf16[8,32,1152]{2,1,0:T(8,128)(2,1)} %broadcast_dynamic-update-slice_fusion), calls=%async_computation | async-start | bytes 1179648 | tf_op jit(solution)/shard_map/all_to_all | solution.py:184
  18.5 1.6 %collective-permute-start.3 = (bf16[18,512]{1,0:T(8,128)(2,1)S(1)}, bf16[18,512]{1,0:T(8,128)(2,1)S(1)}, u32[]{:S(2)}, u32[]{:S(2)}) collective-permute-start(bf16[18,512]{1,0:T(8,128)(2,1)S(1)} %copy-done.6), channel_id=1, source_target_pairs={{0,1},{1,0},{2,3},{3,2},{4,5},{5,4},{6,7},{7,6},{8,9},{9,8},{10,11... | collective-permute-start | bytes 55304 | tf_op jit(solution)/shard_map/ppermute | solution.py:117
  18.8 17.2 %collective-permute-start.1 = (bf16[512,1024]{1,0:T(8,128)(2,1)S(1)}, bf16[512,1024]{1,0:T(8,128)(2,1)}, u32[]{:S(2)}, u32[]{:S(2)}) collective-permute-start(bf16[512,1024]{1,0:T(8,128)(2,1)S(1)} %copy-done.1), channel_id=1, source_target_pairs={{0,1},{1,0},{2,3},{3,2},{4,5},{5,4},{6,7},{7,6},{8,9},{9,8},{10,11... | collective-permute-start | bytes 3145736 | tf_op jit(solution)/shard_map/ppermute | solution.py:117
  19.1 16.9 %collective-permute-start.2 = (bf16[1024,512]{1,0:T(8,128)(2,1)}, bf16[1024,512]{1,0:T(8,128)(2,1)}, u32[]{:S(2)}, u32[]{:S(2)}) collective-permute-start(bf16[1024,512]{1,0:T(8,128)(2,1)} %wh_a.1), channel_id=1, source_target_pairs={{0,1},{1,0},{2,3},{3,2},{4,5},{5,4},{6,7},{7,6},{8,9},{9,8},{10,11... | collective-permute-start | bytes 3145736 | tf_op jit(solution)/shard_map/ppermute | solution.py:117
  19.3 16.7 %collective-permute-start.4 = (bf16[512,1024]{1,0:T(8,128)(2,1)}, bf16[512,1024]{1,0:T(8,128)(2,1)}, u32[]{:S(2)}, u32[]{:S(2)}) collective-permute-start(bf16[512,1024]{1,0:T(8,128)(2,1)} %wo_a.1), channel_id=1, source_target_pairs={{0,1},{1,0},{2,3},{3,2},{4,5},{5,4},{6,7},{7,6},{8,9},{9,8},{10,11... | collective-permute-start | bytes 3145736 | tf_op jit(solution)/shard_map/ppermute | solution.py:117
  36.0 1.2 %copy-start.2 = (bf16[512,1024]{1,0:T(8,128)(2,1)S(1)}, bf16[512,1024]{1,0:T(8,128)(2,1)}, u32[]{:S(2)}) copy-start(bf16[512,1024]{1,0:T(8,128)(2,1)} %r_a.1) | copy-start | bytes 3145732
  51.4 2.9 %collective-permute-start.5 = (bf16[4,256,512]{2,1,0:T(8,128)(2,1)}, bf16[4,256,512]{2,1,0:T(8,128)(2,1)S(1)}, u32[]{:S(2)}, u32[]{:S(2)}) collective-permute-start(bf16[4,256,512]{2,1,0:T(8,128)(2,1)} %get-tuple-element.12), channel_id=1, source_target_pairs={{0,1},{1,0},{2,3},{3,2},{4,5},{5,4},{6,7},{7,6},{8,9},{9,8},{10,11... | collective-permute-start | bytes 3145736 | tf_op jit(solution)/shard_map/ppermute | solution.py:117
  53.3 1.3 %copy-start.3 = (bf16[4,8,16,4,512]{4,3,2,1,0:T(4,128)(2,1)}, bf16[4,8,16,4,512]{4,3,2,1,0:T(4,128)(2,1)S(1)}, u32[]{:S(2)}) copy-start(bf16[4,8,16,4,512]{4,3,2,1,0:T(4,128)(2,1)S(1)} %bitcast_dynamic-update-slice_fusion.1) | copy-start | bytes 6291460

commit v2 on v1

--- a/solution.py
+++ b/solution.py
@@ -262,8 +262,8 @@
             hot = hot_ref[step, rs, :]
             pre_a = dot(normed, wh_a[...]) + dot(hot, emb_ref[:, :half])
             pre_b = dot(normed, wh_b[...]) + dot(hot, emb_ref[:, half:])
-            hid_a = (pre_a * jax.nn.sigmoid(pre_a)).astype(jnp.bfloat16)
-            hid_b = (pre_b * jax.nn.sigmoid(pre_b)).astype(jnp.bfloat16)
+            hid_a = (0.5 * pre_a * (1.0 + jnp.tanh(0.5 * pre_a))).astype(jnp.bfloat16)
+            hid_b = (0.5 * pre_b * (1.0 + jnp.tanh(0.5 * pre_b))).astype(jnp.bfloat16)
             lo = (dot(hid_a, wo_a[:, :half]) + dot(hid_b, wo_b[:, :half])).astype(jnp.bfloat16)
             hi = (dot(hid_a, wo_a[:, half:]) + dot(hid_b, wo_b[:, half:])).astype(jnp.bfloat16)
             keep_ref[step, rs, :] = jnp.where(lead, lo, hi)

time: 56.8 us -> 57 us (level)
  no operation moved by 1% of the time
where the time goes in v2:
time: 57 us; the launch traced here: 56.6 us
  Pallas kernels  17.3 us (30%)
  waiting for transfers between devices  15.9 us (28%)
  starting transfers between devices  8.44 us (15%)
  local copies, waits for them, and re-layouts  7.5 us (13%)
  matrix products  3.72 us (7%)
  other arithmetic  3.52 us (6%)
    all_to_all x1, waiting for transfers between devices, per_device(): got = lax.all_to_all(send, 'tm', split_axis=0, concat_axis=0, tiled=True)  14.9 us
    pallas_call x1, Pallas kernels, imagine(): pl.pallas_call(_imagine_kernel, out_shape=(out, out), in_specs=[pl.BlockS...  14.3 us
    all_to_all x1, starting transfers between devices, per_device(): got = lax.all_to_all(send, 'tm', split_axis=0, concat_axis=0, tiled=True)  6.86 us
    pallas_call x1, Pallas kernels, scan_send(): pl.pallas_call(_scan_send_kernel, out_shape=(jax.ShapeDtypeStruct((ntm, n...  2.97 us
    dot_general x1, matrix products, per_device(): jnp.dot(flat_x, in_proj, preferred_element_type=jnp.float32)  2.47 us
    dynamic_update_slice x1, local copies, waits for them, and re-layouts, per_device(): return lax.dynamic_update_slice(out, theirs, ((1 - m) * bh, 0, 0, 0, 0))  1.84 us
    unnamed x20, local copies, waits for them, and re-layouts  1.64 us
    ppermute x6, starting transfers between devices, partner(): return lax.ppermute(x, 'mp', swap)  1.58 us
  transfers between devices with their start and end apart: 7, of which 2 were waited for; matrix products, arithmetic and copies ran while one was open for 15% of the time, Pallas kernels for 0%

profile of v2, /device:TPU:0, one launch (start us, length us, event | category | flops | bytes accessed | tf_op | source)
XLA Modules:
  0.0 56.6 jit_solution(8359931470403415543)
XLA Ops:
  0.0 0.0 copy-start
  0.0 0.5 collective-permute-start
  0.5 0.8 %fusion.18 = (f32[512]{0:T(512)S(1)}, f32[512]{0:T(512)S(1)}) fusion(f32[1024]{0:T(1024)} %param.14, s32[]{:T(128)S(6)} %select_n.28, s32[]{:T(128)S(6)} %select_n.29), kind=kLoop, calls=%fused_computation.57 | loop fusion | bytes 8200 | tf_op jit(solution)/shard_map/dynamic_slice | solution.py:129
  1.3 1.4 %fusion.14 = (s32[2]{0:T(128)S(1)}, f32[2,128]{1,0:T(2,128)}) fusion(s32[4,128]{1,0:T(4,128)} %param.11, s32[]{:T(128)S(6)} %select_n.27), kind=kLoop, calls=%fused_computation.50 | loop fusion | flops 1278 | bytes 2060 | tf_op jit(solution)/shard_map/reduce_min | solution.py:169
  2.7 0.6 %subtract_sqrt_fusion = (f32[1,1024]{1,0:T(1,128)S(1)}, f32[1,1024]{1,0:T(1,128)}) fusion(f32[1,512]{1,0:T(1,128)S(1)} %bitcast.66, f32[1,512]{1,0:T(1,128)S(1)} %bitcast.65), kind=kLoop, calls=%fused_computation.39 | loop fusion | flops 4096 | bytes 12288 | tf_op jit(solution)/shard_map/sqrt | solution.py:134
  3.3 0.0 copy-done
  3.4 2.5 %convolution_multiply_fusion.1.xa_ref = f32[2,128,512]{2,1,0:T(8,128)} fusion(bf16[1024,512]{1,0:T(8,128)(2,1)} %ip_a.1, bf16[4,128,1024]{2,1,0:T(8,128)(2,1)S(1)} %copy-done, s32[]{:T(128)S(6)} %select_n.27, f32[512]{0:T(512)S(1)} %get-tuple-element.25), kind=kOutput, calls=%fused_computation.1 | convolution fusion | flops 268566528 | bytes 2099204 | tf_op jit(solution)/shard_map/dot_general | solution.py:154
  5.8 0.0 collective-permute-done.ip_b
  5.8 0.0 copy-start.7
  5.9 0.0 copy-start.8
  5.9 1.2 %convolution_multiply_fusion.xb_ref = f32[2,128,512]{2,1,0:T(8,128)} fusion(bf16[1024,512]{1,0:T(8,128)(2,1)S(1)} %collective-permute-done.ip_b, bf16[4,128,1024]{2,1,0:T(8,128)(2,1)S(1)} %copy-done, s32[]{:T(128)S(6)} %select_n.27, f32[512]{0:T(512)S(1)} %get-tuple-element.24), kind=kOutput, calls=%fused_computation | convolution fusion | flops 268566528 | bytes 2099204 | tf_op jit(solution)/shard_map/dot_general | solution.py:157
  7.1 3.0 %shard_map.100 = (bf16[8,32,1152]{2,1,0:T(8,128)(2,1)}, f32[2,1024]{1,0:T(2,128)}) custom-call(f32[2,128]{1,0:T(2,128)} %get-tuple-element.29.keep_ref, f32[1,1024]{1,0:T(1,128)} %get-tuple-element.14.dec_ref, f32[2,128,512]{2,1,0:T(8,128)} %convolution_multiply_fusion.1.xa_ref, f32[2,128,512]{2,1,0:T(8,128)} %convolution_multiply_fusion.xb_ref), custom_call_target="tpu_custom_call" | custom-call | flops 786432 | bytes 1572864 | tf_op jit(solution)/shard_map/pallas_call | solution.py:73
  10.1 0.8 %fusion.8 = (bf16[1,8,2,128]{3,2,1,0:T(2,128)(2,1)S(1)}, bf16[1,8,2,128]{3,2,1,0:T(2,128)(2,1)S(1)}) fusion(f32[2,1024]{1,0:T(2,128)} %get-tuple-element.10), kind=kLoop, calls=%fused_computation.32 | loop fusion | flops 8192 | bytes 16384
  10.9 0.1 concatenate.53
  11.0 0.7 %broadcast_dynamic-update-slice_fusion = bf16[8,32,1152]{2,1,0:T(8,128)(2,1)} fusion(bf16[8,32,1152]{2,1,0:T(8,128)(2,1)} %get-tuple-element.9, bf16[32,128]{1,0:T(8,128)(2,1)S(1)} %bitcast.64), kind=kLoop, calls=%fused_computation.27 | loop fusion | bytes 73728 | tf_op jit(solution)/shard_map/dynamic_update_slice | solution.py:181
  11.6 6.9 %all-to-all-start = ((bf16[8,32,1152]{2,1,0:T(8,128)(2,1)}), bf16[8,32,1152]{2,1,0:T(8,128)(2,1)S(1)}, u32[]{:S(2)}, u32[]{:S(2)}) async-start(bf16[8,32,1152]{2,1,0:T(8,128)(2,1)} %broadcast_dynamic-update-slice_fusion), calls=%async_computation | async-start | bytes 1179648 | tf_op jit(solution)/shard_map/all_to_all | solution.py:184
  18.5 0.2 collective-permute-start.3
  18.8 0.3 collective-permute-start.1
  19.1 0.2 collective-permute-start.2
  19.3 0.3 collective-permute-start.4
  19.6 0.1 reshape.171
  19.7 0.1 broadcast_power_fusion
  19.8 0.2 fusion.4.hot_ref
  20.1 0.0 copy-done.5
  20.1 0.0 copy-done.8
  20.1 0.0 collective-permute-done.3
  20.1 14.9 %all-to-all-done = bf16[8,32,1152]{2,1,0:T(8,128)(2,1)S(1)} async-done(((bf16[8,32,1152]{2,1,0:T(8,128)(2,1)}), bf16[8,32,1152]{2,1,0:T(8,128)(2,1)S(1)}, u32[]{:S(2)}, u32[]{:S(2)}) %all-to-all-start) | async-done | bytes 589856 | tf_op jit(solution)/shard_map/all_to_all | solution.py:184
  35.1 0.1 slice.67
  35.2 0.1 copy.19
  35.2 0.1 copy.18
  35.3 0.1 broadcast_multiply_fusion
  35.4 0.1 multiply_add_fusion
  35.5 0.1 slice.61
  35.7 0.1 broadcast_compare_fusion
  35.7 0.2 bitcast_add_fusion
  36.0 0.0 collective-permute-done.1.r_b
  36.0 0.0 collective-permute-done.2.wh_b
  36.0 0.0 collective-permute-done.4.wo_b
  36.0 0.0 copy-start.2
  36.0 1.2 %copy-done.2 = bf16[512,1024]{1,0:T(8,128)(2,1)S(1)} copy-done((bf16[512,1024]{1,0:T(8,128)(2,1)S(1)}, bf16[512,1024]{1,0:T(8,128)(2,1)}, u32[]{:S(2)}) %copy-start.2) | copy-done | bytes 1048600
  37.2 14.3 %shard_map.101 = (bf16[4,256,512]{2,1,0:T(8,128)(2,1)S(1)}, bf16[4,256,512]{2,1,0:T(8,128)(2,1)}) custom-call(s32[1]{0:T(128)} %bitcast.side_ref, f32[256,1024]{1,0:T(8,128)S(1)} %bitcast.52, bf16[4,256,128]{2,1,0:T(8,128)(2,1)S(1)} %fusion.4.hot_ref, f32[3,1024]{1,0:T(4,128)S(1)} %pad_maximum_fusion.vec_ref, bf16[512,1024]{1,0:T(8,128)(2,1)S(1)} %copy-done.2, ...), custom_call_target="tpu_custom_call" | custom-call | flops 8589934592 | bytes 16777216 | tf_op jit(solution)/shard_map/pallas_call | solution.py:287
  51.5 0.0 collective-permute-start.5
  51.5 0.9 %broadcast_in_dim.38 = bf16[4,8,16,4,512]{4,3,2,1,0:T(4,128)(2,1)S(1)} broadcast(bf16[]{:T(256)} %constant.15.clone.1), dimensions={} | broadcast | bytes 2097154 | tf_op jit(solution)/shard_map/broadcast_in_dim | solution.py:234
  52.5 0.9 %bitcast_dynamic-update-slice_fusion.1 = bf16[4,8,16,4,512]{4,3,2,1,0:T(4,128)(2,1)S(1)} fusion(bf16[4,8,16,4,512]{4,3,2,1,0:T(4,128)(2,1)S(1)} %broadcast_in_dim.38, s32[]{:T(128)S(6)} %select_n.27, bf16[4,2,8,16,512]{4,3,2,1,0:T(8,128)(2,1)S(1)} %bitcast.51), kind=kLoop, calls=%fused_computation.3 | loop fusion | bytes 2097156 | tf_op jit(solution)/shard_map/dynamic_update_slice | solution.py:235
  53.4 0.0 copy-start.3
  53.4 1.0 %collective-permute-done.5 = bf16[4,256,512]{2,1,0:T(8,128)(2,1)S(1)} collective-permute-done((bf16[4,256,512]{2,1,0:T(8,128)(2,1)}, bf16[4,256,512]{2,1,0:T(8,128)(2,1)S(1)}, u32[]{:S(2)}, u32[]{:S(2)}) %collective-permute-start.5) | collective-permute-done | bytes 1048608 | tf_op jit(solution)/shard_map/ppermute | solution.py:117
  54.4 0.3 copy-done.3
  54.7 1.8 %bitcast_dynamic-update-slice_fusion = bf16[4,8,16,4,512]{4,3,2,1,0:T(4,128)(2,1)} fusion(bf16[4,8,16,4,512]{4,3,2,1,0:T(4,128)(2,1)} %copy-done.3, s32[]{:T(128)S(6)} %select_n.33, bf16[4,2,8,16,512]{4,3,2,1,0:T(8,128)(2,1)S(1)} %bitcast.54), kind=kLoop, calls=%fused_computation.2 | loop fusion | bytes 2097156 | tf_op jit(solution)/shard_map/dynamic_update_slice | solution.py:236
  (25 shorter events, 0.2 us)
Async XLA Ops:
  0.0 3.3 %copy-start = (bf16[4,128,1024]{2,1,0:T(8,128)(2,1)S(1)}, bf16[4,128,1024]{2,1,0:T(8,128)(2,1)}, u32[]{:S(2)}) copy-start(bf16[4,128,1024]{2,1,0:T(8,128)(2,1)} %param.10) | copy-start | bytes 3145732
  0.0 5.8 %collective-permute-start = (bf16[1024,512]{1,0:T(8,128)(2,1)}, bf16[1024,512]{1,0:T(8,128)(2,1)S(1)}, u32[]{:S(2)}, u32[]{:S(2)}) collective-permute-start(bf16[1024,512]{1,0:T(8,128)(2,1)} %ip_a.1), channel_id=1, source_target_pairs={{0,1},{1,0},{2,3},{3,2},{4,5},{5,4},{6,7},{7,6},{8,9},{9,8},{10,11... | collective-permute-start | bytes 3145736 | tf_op jit(solution)/shard_map/ppermute | solution.py:117
  5.8 5.8 %copy-start.4 = (bf16[1024,512]{1,0:T(8,128)(2,1)}, bf16[1024,512]{1,0:T(8,128)(2,1)S(1)}, u32[]{:S(2)}) copy-start(bf16[1024,512]{1,0:T(8,128)(2,1)S(1)} %collective-permute-done.ip_b) | copy-start | bytes 3145732
  5.8 12.7 %copy-start.6 = (bf16[18,512]{1,0:T(8,128)(2,1)S(1)}, bf16[18,512]{1,0:T(8,128)(2,1)}, u32[]{:S(2)}) copy-start(bf16[18,512]{1,0:T(8,128)(2,1)} %param.18) | copy-start | bytes 55300
  5.8 12.9 %copy-start.1 = (bf16[512,1024]{1,0:T(8,128)(2,1)S(1)}, bf16[512,1024]{1,0:T(8,128)(2,1)}, u32[]{:S(2)}) copy-start(bf16[512,1024]{1,0:T(8,128)(2,1)} %r_a.1) | copy-start | bytes 3145732
  5.8 13.8 %copy-start.7 = (s32[4,8,16,4]{2,3,1,0:T(4,128)S(1)}, s32[4,8,16,4]{2,3,1,0:T(4,128)}, u32[]{:S(2)}) copy-start(s32[4,8,16,4]{2,3,1,0:T(4,128)} %param.12) | copy-start | bytes 24580
  5.8 14.2 %copy-start.5 = (f32[1,1024]{1,0:T(1,128)S(1)}, f32[1,1024]{1,0:T(1,128)}, u32[]{:S(2)}) copy-start(f32[1,1024]{1,0:T(1,128)} %get-tuple-element.14.dec_ref) | copy-start | bytes 12292
  5.9 14.2 %copy-start.8 = (f32[1024]{0:T(1024)S(1)}, f32[1024]{0:T(1024)}, u32[]{:S(2)}) copy-start(f32[1024]{0:T(1024)} %param.16) | copy-start | bytes 12292
  11.6 23.4 %all-to-all-start = ((bf16[8,32,1152]{2,1,0:T(8,128)(2,1)}), bf16[8,32,1152]{2,1,0:T(8,128)(2,1)S(1)}, u32[]{:S(2)}, u32[]{:S(2)}) async-start(bf16[8,32,1152]{2,1,0:T(8,128)(2,1)} %broadcast_dynamic-update-slice_fusion), calls=%async_computation | async-start | bytes 1179648 | tf_op jit(solution)/shard_map/all_to_all | solution.py:184
  18.5 1.6 %collective-permute-start.3 = (bf16[18,512]{1,0:T(8,128)(2,1)S(1)}, bf16[18,512]{1,0:T(8,128)(2,1)S(1)}, u32[]{:S(2)}, u32[]{:S(2)}) collective-permute-start(bf16[18,512]{1,0:T(8,128)(2,1)S(1)} %copy-done.6), channel_id=1, source_target_pairs={{0,1},{1,0},{2,3},{3,2},{4,5},{5,4},{6,7},{7,6},{8,9},{9,8},{10,11... | collective-permute-start | bytes 55304 | tf_op jit(solution)/shard_map/ppermute | solution.py:117
  18.8 17.2 %collective-permute-start.1 = (bf16[512,1024]{1,0:T(8,128)(2,1)S(1)}, bf16[512,1024]{1,0:T(8,128)(2,1)}, u32[]{:S(2)}, u32[]{:S(2)}) collective-permute-start(bf16[512,1024]{1,0:T(8,128)(2,1)S(1)} %copy-done.1), channel_id=1, source_target_pairs={{0,1},{1,0},{2,3},{3,2},{4,5},{5,4},{6,7},{7,6},{8,9},{9,8},{10,11... | collective-permute-start | bytes 3145736 | tf_op jit(solution)/shard_map/ppermute | solution.py:117
  19.1 16.9 %collective-permute-start.2 = (bf16[1024,512]{1,0:T(8,128)(2,1)}, bf16[1024,512]{1,0:T(8,128)(2,1)}, u32[]{:S(2)}, u32[]{:S(2)}) collective-permute-start(bf16[1024,512]{1,0:T(8,128)(2,1)} %wh_a.1), channel_id=1, source_target_pairs={{0,1},{1,0},{2,3},{3,2},{4,5},{5,4},{6,7},{7,6},{8,9},{9,8},{10,11... | collective-permute-start | bytes 3145736 | tf_op jit(solution)/shard_map/ppermute | solution.py:117
  19.3 16.7 %collective-permute-start.4 = (bf16[512,1024]{1,0:T(8,128)(2,1)}, bf16[512,1024]{1,0:T(8,128)(2,1)}, u32[]{:S(2)}, u32[]{:S(2)}) collective-permute-start(bf16[512,1024]{1,0:T(8,128)(2,1)} %wo_a.1), channel_id=1, source_target_pairs={{0,1},{1,0},{2,3},{3,2},{4,5},{5,4},{6,7},{7,6},{8,9},{9,8},{10,11... | collective-permute-start | bytes 3145736 | tf_op jit(solution)/shard_map/ppermute | solution.py:117
  36.0 1.2 %copy-start.2 = (bf16[512,1024]{1,0:T(8,128)(2,1)S(1)}, bf16[512,1024]{1,0:T(8,128)(2,1)}, u32[]{:S(2)}) copy-start(bf16[512,1024]{1,0:T(8,128)(2,1)} %r_a.1) | copy-start | bytes 3145732
  51.5 2.9 %collective-permute-start.5 = (bf16[4,256,512]{2,1,0:T(8,128)(2,1)}, bf16[4,256,512]{2,1,0:T(8,128)(2,1)S(1)}, u32[]{:S(2)}, u32[]{:S(2)}) collective-permute-start(bf16[4,256,512]{2,1,0:T(8,128)(2,1)} %get-tuple-element.12), channel_id=1, source_target_pairs={{0,1},{1,0},{2,3},{3,2},{4,5},{5,4},{6,7},{7,6},{8,9},{9,8},{10,11... | collective-permute-start | bytes 3145736 | tf_op jit(solution)/shard_map/ppermute | solution.py:117
  53.4 1.3 %copy-start.3 = (bf16[4,8,16,4,512]{4,3,2,1,0:T(4,128)(2,1)}, bf16[4,8,16,4,512]{4,3,2,1,0:T(4,128)(2,1)S(1)}, u32[]{:S(2)}) copy-start(bf16[4,8,16,4,512]{4,3,2,1,0:T(4,128)(2,1)S(1)} %bitcast_dynamic-update-slice_fusion.1) | copy-start | bytes 6291460

commit v3 on v1

--- a/solution.py
+++ b/solution.py
@@ -54,7 +54,7 @@
         return tuple(new)
 
     start = tuple(jnp.zeros((1, half), jnp.float32) for _ in range(2 * nb))
-    final = lax.fori_loop(0, steps, body, start, unroll=8)
+    final = lax.fori_loop(0, steps, body, start, unroll=16)
     for b in range(nb):
         ends_ref[pl.ds(b, 1), pl.ds(0, half)] = final[2 * b]
         ends_ref[pl.ds(b, 1), pl.ds(half, half)] = final[2 * b + 1]

time: 56.8 us -> 56.9 us (level)
  no operation moved by 1% of the time
where the time goes in v3:
time: 56.9 us; the launch traced here: 56.5 us
  Pallas kernels  17.2 us (30%)
  waiting for transfers between devices  15.9 us (28%)
  starting transfers between devices  8.44 us (15%)
  local copies, waits for them, and re-layouts  7.5 us (13%)
  matrix products  3.72 us (7%)
  other arithmetic  3.52 us (6%)
    all_to_all x1, waiting for transfers between devices, per_device(): got = lax.all_to_all(send, 'tm', split_axis=0, concat_axis=0, tiled=True)  14.9 us
    pallas_call x1, Pallas kernels, imagine(): pl.pallas_call(_imagine_kernel, out_shape=(out, out), in_specs=[pl.BlockS...  14.2 us
    all_to_all x1, starting transfers between devices, per_device(): got = lax.all_to_all(send, 'tm', split_axis=0, concat_axis=0, tiled=True)  6.86 us
    pallas_call x1, Pallas kernels, scan_send(): pl.pallas_call(_scan_send_kernel, out_shape=(jax.ShapeDtypeStruct((ntm, n...  3.02 us
    dot_general x1, matrix products, per_device(): jnp.dot(flat_x, in_proj, preferred_element_type=jnp.float32)  2.47 us
    dynamic_update_slice x1, local copies, waits for them, and re-layouts, per_device(): return lax.dynamic_update_slice(out, theirs, ((1 - m) * bh, 0, 0, 0, 0))  1.84 us
    unnamed x20, local copies, waits for them, and re-layouts  1.64 us
    ppermute x6, starting transfers between devices, partner(): return lax.ppermute(x, 'mp', swap)  1.58 us
  transfers between devices with their start and end apart: 7, of which 2 were waited for; matrix products, arithmetic and copies ran while one was open for 15% of the time, Pallas kernels for 0%

profile of v3, /device:TPU:0, one launch (start us, length us, event | category | flops | bytes accessed | tf_op | source)
XLA Modules:
  0.0 56.5 jit_solution(18219283723170228425)
XLA Ops:
  0.0 0.5 collective-permute-start
  0.5 0.8 %fusion.18 = (f32[512]{0:T(512)S(1)}, f32[512]{0:T(512)S(1)}) fusion(f32[1024]{0:T(1024)} %param.14, s32[]{:T(128)S(6)} %select_n.28, s32[]{:T(128)S(6)} %select_n.29), kind=kLoop, calls=%fused_computation.57 | loop fusion | bytes 8200 | tf_op jit(solution)/shard_map/dynamic_slice | solution.py:129
  1.3 1.4 %fusion.14 = (s32[2]{0:T(128)S(1)}, f32[2,128]{1,0:T(2,128)}) fusion(s32[4,128]{1,0:T(4,128)} %param.11, s32[]{:T(128)S(6)} %select_n.27), kind=kLoop, calls=%fused_computation.50 | loop fusion | flops 1278 | bytes 2060 | tf_op jit(solution)/shard_map/reduce_min | solution.py:169
  2.7 0.6 %subtract_sqrt_fusion = (f32[1,1024]{1,0:T(1,128)S(1)}, f32[1,1024]{1,0:T(1,128)}) fusion(f32[1,512]{1,0:T(1,128)S(1)} %bitcast.66, f32[1,512]{1,0:T(1,128)S(1)} %bitcast.65), kind=kLoop, calls=%fused_computation.39 | loop fusion | flops 4096 | bytes 12288 | tf_op jit(solution)/shard_map/sqrt | solution.py:134
  3.3 0.0 copy-done
  3.4 2.5 %convolution_multiply_fusion.1.xa_ref = f32[2,128,512]{2,1,0:T(8,128)} fusion(bf16[1024,512]{1,0:T(8,128)(2,1)} %ip_a.1, bf16[4,128,1024]{2,1,0:T(8,128)(2,1)S(1)} %copy-done, s32[]{:T(128)S(6)} %select_n.27, f32[512]{0:T(512)S(1)} %get-tuple-element.25), kind=kOutput, calls=%fused_computation.1 | convolution fusion | flops 268566528 | bytes 2099204 | tf_op jit(solution)/shard_map/dot_general | solution.py:154
  5.8 0.0 collective-permute-done.ip_b
  5.8 0.0 copy-start.7
  5.9 0.0 copy-start.8
  5.9 1.2 %convolution_multiply_fusion.xb_ref = f32[2,128,512]{2,1,0:T(8,128)} fusion(bf16[1024,512]{1,0:T(8,128)(2,1)S(1)} %collective-permute-done.ip_b, bf16[4,128,1024]{2,1,0:T(8,128)(2,1)S(1)} %copy-done, s32[]{:T(128)S(6)} %select_n.27, f32[512]{0:T(512)S(1)} %get-tuple-element.24), kind=kOutput, calls=%fused_computation | convolution fusion | flops 268566528 | bytes 2099204 | tf_op jit(solution)/shard_map/dot_general | solution.py:157
  7.1 3.0 %shard_map.100 = (bf16[8,32,1152]{2,1,0:T(8,128)(2,1)}, f32[2,1024]{1,0:T(2,128)}) custom-call(f32[2,128]{1,0:T(2,128)} %get-tuple-element.29.keep_ref, f32[1,1024]{1,0:T(1,128)} %get-tuple-element.14.dec_ref, f32[2,128,512]{2,1,0:T(8,128)} %convolution_multiply_fusion.1.xa_ref, f32[2,128,512]{2,1,0:T(8,128)} %convolution_multiply_fusion.xb_ref), custom_call_target="tpu_custom_call" | custom-call | flops 786432 | bytes 1572864 | tf_op jit(solution)/shard_map/pallas_call | solution.py:73
  10.1 0.8 %fusion.8 = (bf16[1,8,2,128]{3,2,1,0:T(2,128)(2,1)S(1)}, bf16[1,8,2,128]{3,2,1,0:T(2,128)(2,1)S(1)}) fusion(f32[2,1024]{1,0:T(2,128)} %get-tuple-element.10), kind=kLoop, calls=%fused_computation.32 | loop fusion | flops 8192 | bytes 16384
  10.9 0.1 concatenate.53
  11.0 0.7 %broadcast_dynamic-update-slice_fusion = bf16[8,32,1152]{2,1,0:T(8,128)(2,1)} fusion(bf16[8,32,1152]{2,1,0:T(8,128)(2,1)} %get-tuple-element.9, bf16[32,128]{1,0:T(8,128)(2,1)S(1)} %bitcast.64), kind=kLoop, calls=%fused_computation.27 | loop fusion | bytes 73728 | tf_op jit(solution)/shard_map/dynamic_update_slice | solution.py:181
  11.7 0.0 copy-done.4
  11.7 6.9 %all-to-all-start = ((bf16[8,32,1152]{2,1,0:T(8,128)(2,1)}), bf16[8,32,1152]{2,1,0:T(8,128)(2,1)S(1)}, u32[]{:S(2)}, u32[]{:S(2)}) async-start(bf16[8,32,1152]{2,1,0:T(8,128)(2,1)} %broadcast_dynamic-update-slice_fusion), calls=%async_computation | async-start | bytes 1179648 | tf_op jit(solution)/shard_map/all_to_all | solution.py:184
  18.5 0.2 collective-permute-start.3
  18.8 0.0 copy-done.1
  18.8 0.3 collective-permute-start.1
  19.1 0.2 collective-permute-start.2
  19.3 0.3 collective-permute-start.4
  19.6 0.0 copy-done.7
  19.6 0.1 reshape.171
  19.7 0.1 broadcast_power_fusion
  19.9 0.2 fusion.4.hot_ref
  20.1 0.0 collective-permute-done.3
  20.2 14.9 %all-to-all-done = bf16[8,32,1152]{2,1,0:T(8,128)(2,1)S(1)} async-done(((bf16[8,32,1152]{2,1,0:T(8,128)(2,1)}), bf16[8,32,1152]{2,1,0:T(8,128)(2,1)S(1)}, u32[]{:S(2)}, u32[]{:S(2)}) %all-to-all-start) | async-done | bytes 589856 | tf_op jit(solution)/shard_map/all_to_all | solution.py:184
  35.1 0.1 slice.67
  35.2 0.1 copy.19
  35.3 0.1 copy.18
  35.4 0.1 broadcast_multiply_fusion
  35.5 0.1 multiply_add_fusion
  35.6 0.1 slice.61
  35.7 0.1 broadcast_compare_fusion
  35.8 0.2 bitcast_add_fusion
  36.0 0.0 collective-permute-done.1.r_b
  36.0 0.0 collective-permute-done.2.wh_b
  36.0 0.0 collective-permute-done.4.wo_b
  36.0 0.0 copy-start.2
  36.0 1.2 %copy-done.2 = bf16[512,1024]{1,0:T(8,128)(2,1)S(1)} copy-done((bf16[512,1024]{1,0:T(8,128)(2,1)S(1)}, bf16[512,1024]{1,0:T(8,128)(2,1)}, u32[]{:S(2)}) %copy-start.2) | copy-done | bytes 1048600
  37.3 14.2 %shard_map.101 = (bf16[4,256,512]{2,1,0:T(8,128)(2,1)S(1)}, bf16[4,256,512]{2,1,0:T(8,128)(2,1)}) custom-call(s32[1]{0:T(128)} %bitcast.side_ref, f32[256,1024]{1,0:T(8,128)S(1)} %bitcast.52, bf16[4,256,128]{2,1,0:T(8,128)(2,1)S(1)} %fusion.4.hot_ref, f32[3,1024]{1,0:T(4,128)S(1)} %pad_maximum_fusion.vec_ref, bf16[512,1024]{1,0:T(8,128)(2,1)S(1)} %copy-done.2, ...), custom_call_target="tpu_custom_call" | custom-call | flops 8589934592 | bytes 16777216 | tf_op jit(solution)/shard_map/pallas_call | solution.py:287
  51.4 0.0 collective-permute-start.5
  51.4 0.9 %broadcast_in_dim.38 = bf16[4,8,16,4,512]{4,3,2,1,0:T(4,128)(2,1)S(1)} broadcast(bf16[]{:T(256)} %constant.15.clone.1), dimensions={} | broadcast | bytes 2097154 | tf_op jit(solution)/shard_map/broadcast_in_dim | solution.py:234
  52.4 0.9 %bitcast_dynamic-update-slice_fusion.1 = bf16[4,8,16,4,512]{4,3,2,1,0:T(4,128)(2,1)S(1)} fusion(bf16[4,8,16,4,512]{4,3,2,1,0:T(4,128)(2,1)S(1)} %broadcast_in_dim.38, s32[]{:T(128)S(6)} %select_n.27, bf16[4,2,8,16,512]{4,3,2,1,0:T(8,128)(2,1)S(1)} %bitcast.51), kind=kLoop, calls=%fused_computation.3 | loop fusion | bytes 2097156 | tf_op jit(solution)/shard_map/dynamic_update_slice | solution.py:235
  53.3 0.0 copy-start.3
  53.3 1.0 %collective-permute-done.5 = bf16[4,256,512]{2,1,0:T(8,128)(2,1)S(1)} collective-permute-done((bf16[4,256,512]{2,1,0:T(8,128)(2,1)}, bf16[4,256,512]{2,1,0:T(8,128)(2,1)S(1)}, u32[]{:S(2)}, u32[]{:S(2)}) %collective-permute-start.5) | collective-permute-done | bytes 1048608 | tf_op jit(solution)/shard_map/ppermute | solution.py:117
  54.3 0.3 copy-done.3
  54.7 1.8 %bitcast_dynamic-update-slice_fusion = bf16[4,8,16,4,512]{4,3,2,1,0:T(4,128)(2,1)} fusion(bf16[4,8,16,4,512]{4,3,2,1,0:T(4,128)(2,1)} %copy-done.3, s32[]{:T(128)S(6)} %select_n.33, bf16[4,2,8,16,512]{4,3,2,1,0:T(8,128)(2,1)S(1)} %bitcast.54), kind=kLoop, calls=%fused_computation.2 | loop fusion | bytes 2097156 | tf_op jit(solution)/shard_map/dynamic_update_slice | solution.py:236
  (25 shorter events, 0.2 us)
Async XLA Ops:
  0.0 3.3 %copy-start = (bf16[4,128,1024]{2,1,0:T(8,128)(2,1)S(1)}, bf16[4,128,1024]{2,1,0:T(8,128)(2,1)}, u32[]{:S(2)}) copy-start(bf16[4,128,1024]{2,1,0:T(8,128)(2,1)} %param.10) | copy-start | bytes 3145732
  0.0 5.8 %collective-permute-start = (bf16[1024,512]{1,0:T(8,128)(2,1)}, bf16[1024,512]{1,0:T(8,128)(2,1)S(1)}, u32[]{:S(2)}, u32[]{:S(2)}) collective-permute-start(bf16[1024,512]{1,0:T(8,128)(2,1)} %ip_a.1), channel_id=1, source_target_pairs={{0,1},{1,0},{2,3},{3,2},{4,5},{5,4},{6,7},{7,6},{8,9},{9,8},{10,11... | collective-permute-start | bytes 3145736 | tf_op jit(solution)/shard_map/ppermute | solution.py:117
  5.8 5.8 %copy-start.4 = (bf16[1024,512]{1,0:T(8,128)(2,1)}, bf16[1024,512]{1,0:T(8,128)(2,1)S(1)}, u32[]{:S(2)}) copy-start(bf16[1024,512]{1,0:T(8,128)(2,1)S(1)} %collective-permute-done.ip_b) | copy-start | bytes 3145732
  5.8 12.7 %copy-start.6 = (bf16[18,512]{1,0:T(8,128)(2,1)S(1)}, bf16[18,512]{1,0:T(8,128)(2,1)}, u32[]{:S(2)}) copy-start(bf16[18,512]{1,0:T(8,128)(2,1)} %param.18) | copy-start | bytes 55300
  5.8 13.0 %copy-start.1 = (bf16[512,1024]{1,0:T(8,128)(2,1)S(1)}, bf16[512,1024]{1,0:T(8,128)(2,1)}, u32[]{:S(2)}) copy-start(bf16[512,1024]{1,0:T(8,128)(2,1)} %r_a.1) | copy-start | bytes 3145732
  5.8 13.8 %copy-start.7 = (s32[4,8,16,4]{2,3,1,0:T(4,128)S(1)}, s32[4,8,16,4]{2,3,1,0:T(4,128)}, u32[]{:S(2)}) copy-start(s32[4,8,16,4]{2,3,1,0:T(4,128)} %param.12) | copy-start | bytes 24580
  5.8 14.3 %copy-start.5 = (f32[1,1024]{1,0:T(1,128)S(1)}, f32[1,1024]{1,0:T(1,128)}, u32[]{:S(2)}) copy-start(f32[1,1024]{1,0:T(1,128)} %get-tuple-element.14.dec_ref) | copy-start | bytes 12292
  5.9 14.3 %copy-start.8 = (f32[1024]{0:T(1024)S(1)}, f32[1024]{0:T(1024)}, u32[]{:S(2)}) copy-start(f32[1024]{0:T(1024)} %param.16) | copy-start | bytes 12292
  11.7 23.4 %all-to-all-start = ((bf16[8,32,1152]{2,1,0:T(8,128)(2,1)}), bf16[8,32,1152]{2,1,0:T(8,128)(2,1)S(1)}, u32[]{:S(2)}, u32[]{:S(2)}) async-start(bf16[8,32,1152]{2,1,0:T(8,128)(2,1)} %broadcast_dynamic-update-slice_fusion), calls=%async_computation | async-start | bytes 1179648 | tf_op jit(solution)/shard_map/all_to_all | solution.py:184
  18.5 1.6 %collective-permute-start.3 = (bf16[18,512]{1,0:T(8,128)(2,1)S(1)}, bf16[18,512]{1,0:T(8,128)(2,1)S(1)}, u32[]{:S(2)}, u32[]{:S(2)}) collective-permute-start(bf16[18,512]{1,0:T(8,128)(2,1)S(1)} %copy-done.6), channel_id=1, source_target_pairs={{0,1},{1,0},{2,3},{3,2},{4,5},{5,4},{6,7},{7,6},{8,9},{9,8},{10,11... | collective-permute-start | bytes 55304 | tf_op jit(solution)/shard_map/ppermute | solution.py:117
  18.8 17.2 %collective-permute-start.1 = (bf16[512,1024]{1,0:T(8,128)(2,1)S(1)}, bf16[512,1024]{1,0:T(8,128)(2,1)}, u32[]{:S(2)}, u32[]{:S(2)}) collective-permute-start(bf16[512,1024]{1,0:T(8,128)(2,1)S(1)} %copy-done.1), channel_id=1, source_target_pairs={{0,1},{1,0},{2,3},{3,2},{4,5},{5,4},{6,7},{7,6},{8,9},{9,8},{10,11... | collective-permute-start | bytes 3145736 | tf_op jit(solution)/shard_map/ppermute | solution.py:117
  19.1 16.9 %collective-permute-start.2 = (bf16[1024,512]{1,0:T(8,128)(2,1)}, bf16[1024,512]{1,0:T(8,128)(2,1)}, u32[]{:S(2)}, u32[]{:S(2)}) collective-permute-start(bf16[1024,512]{1,0:T(8,128)(2,1)} %wh_a.1), channel_id=1, source_target_pairs={{0,1},{1,0},{2,3},{3,2},{4,5},{5,4},{6,7},{7,6},{8,9},{9,8},{10,11... | collective-permute-start | bytes 3145736 | tf_op jit(solution)/shard_map/ppermute | solution.py:117
  19.3 16.7 %collective-permute-start.4 = (bf16[512,1024]{1,0:T(8,128)(2,1)}, bf16[512,1024]{1,0:T(8,128)(2,1)}, u32[]{:S(2)}, u32[]{:S(2)}) collective-permute-start(bf16[512,1024]{1,0:T(8,128)(2,1)} %wo_a.1), channel_id=1, source_target_pairs={{0,1},{1,0},{2,3},{3,2},{4,5},{5,4},{6,7},{7,6},{8,9},{9,8},{10,11... | collective-permute-start | bytes 3145736 | tf_op jit(solution)/shard_map/ppermute | solution.py:117
  36.0 1.2 %copy-start.2 = (bf16[512,1024]{1,0:T(8,128)(2,1)S(1)}, bf16[512,1024]{1,0:T(8,128)(2,1)}, u32[]{:S(2)}) copy-start(bf16[512,1024]{1,0:T(8,128)(2,1)} %r_a.1) | copy-start | bytes 3145732
  51.4 2.9 %collective-permute-start.5 = (bf16[4,256,512]{2,1,0:T(8,128)(2,1)}, bf16[4,256,512]{2,1,0:T(8,128)(2,1)S(1)}, u32[]{:S(2)}, u32[]{:S(2)}) collective-permute-start(bf16[4,256,512]{2,1,0:T(8,128)(2,1)} %get-tuple-element.12), channel_id=1, source_target_pairs={{0,1},{1,0},{2,3},{3,2},{4,5},{5,4},{6,7},{7,6},{8,9},{9,8},{10,11... | collective-permute-start | bytes 3145736 | tf_op jit(solution)/shard_map/ppermute | solution.py:117
  53.3 1.3 %copy-start.3 = (bf16[4,8,16,4,512]{4,3,2,1,0:T(4,128)(2,1)}, bf16[4,8,16,4,512]{4,3,2,1,0:T(4,128)(2,1)S(1)}, u32[]{:S(2)}) copy-start(bf16[4,8,16,4,512]{4,3,2,1,0:T(4,128)(2,1)S(1)} %bitcast_dynamic-update-slice_fusion.1) | copy-start | bytes 6291460
